TPU v7x, 512 devices: a whole 4x4x16 slice. The times are simulated.
512 devices in a mesh: attn: 64 (over y, z), dp: 4 (over x), tensor: 2 (over core).
Axes of the slice: x: 4, y: 4, z: 16, core: 2. Of those that a mesh axis runs over, the one named last changes fastest.
Arguments:
- hidden_state: bfloat16 [256, 8192], P('dp', 'attn'), may hold values from -6 to 6
- w_query: bfloat16 [8192, 8192], P('attn', 'tensor'), may hold values from -0.0625 to 0.0625
- w_keyval: bfloat16 [8192, 2, 1024], P('attn', None, 'tensor'), may hold values from -0.0625 to 0.0625
- w_output: bfloat16 [8192, 8192], P('tensor', 'attn'), may hold values from -0.0625 to 0.0625
- kv_cache: bfloat16 [4, 49152, 2, 8, 128], P('dp', 'attn', None, 'tensor'), as said below
- lengths: int32 [4, 64], P('dp'), may hold values from 1 to 256, 8192 in all within a row
- owner_of: int32 [4, 64, 1], P('dp'), may hold values from 0 to 63; in each aligned block of 64 rows (0 to 63, 64 to 127, ..., all dimensions but the last counted through in order) at most 3 rows name the same one
Outputs:
- attended: bfloat16 [256, 8192], P('dp', 'attn')
Inputs may be any that keep to these rules, and one draw needn't show every extreme that they name: `owner_of`: in each data group at most 3 requests are placed on one attention device, and in some groups exactly 3 on one. The lengths of each data group sum to 8192, and the longest is exactly 256. `kv_cache`: finite keys and values.
All inputs are finite; a program needn't handle non-finite values.
Results may differ from a plain program's by a relative error of at most 0.009.
The roundings to bfloat16 on the way count: a program that leaves them out, or rounds other values in their place, can miss the bound.
Values may be sent and summed in bfloat16 or wider, within the bound.
No kernel may reach another device: no remote copies, remote signals or barrier semaphores. Data moves between devices by JAX's collectives and lax.ppermute only.
A program may use at most 64 MiB of HBM per device.

v0:
```python
import math
import jax
import jax.numpy as jnp
from jax import lax
from jax.sharding import PartitionSpec as P

HD = 128
CAP = 3
ROPE_BASE = 500000.0


def rotate_pairs(vectors, positions):
    half_dim = vectors.shape[-1] // 2
    steps_f = jnp.arange(half_dim).astype(jnp.float32) * (2.0 / vectors.shape[-1])
    inv_freq = jnp.exp(-math.log(ROPE_BASE) * steps_f)
    angles = positions[:, None] * inv_freq[None, :]
    cosine = jnp.cos(angles)[:, None, :]
    sine_part = jnp.sin(angles)[:, None, :]
    front_half = vectors[..., :half_dim]
    back_half = vectors[..., half_dim:]
    return jnp.concatenate(
        [front_half * cosine - back_half * sine_part, back_half * cosine + front_half * sine_part],
        axis=-1,
    )


def finish(query_part, keyval_part, positions, heads_loc, kv_loc):
    row_count = query_part.shape[0]
    query_rot = rotate_pairs(query_part.reshape(row_count, heads_loc, HD), positions).astype(
        jnp.bfloat16
    )
    keyval = keyval_part.reshape(row_count, 2, kv_loc, HD)
    key_rot = rotate_pairs(keyval[:, 0], positions).astype(jnp.bfloat16)
    val_new = keyval[:, 1].astype(jnp.bfloat16)
    packed = jnp.stack([key_rot, val_new], axis=1).reshape(row_count, 2 * kv_loc * HD)
    return (query_rot.reshape(row_count, heads_loc * HD), packed)


def local(hidden_state, w_query, w_keyval, w_output, kv_cache, lengths, owner_of):
    rows_group = hidden_state.shape[0]
    width_loc = hidden_state.shape[1]
    my_index = lax.axis_index("attn")
    heads_loc = w_query.shape[1] // HD
    kv_loc = w_keyval.shape[2] // HD
    group_size = heads_loc // kv_loc
    score_scale = 1.0 / math.sqrt(HD)
    query_part = jnp.dot(hidden_state, w_query, preferred_element_type=jnp.float32)
    keyval_part = jnp.dot(
        hidden_state,
        w_keyval.reshape(width_loc, 2 * kv_loc * HD),
        preferred_element_type=jnp.float32,
    )
    owners = owner_of.reshape(rows_group)
    req_lens = lengths.reshape(rows_group)
    req_order = jnp.arange(rows_group, dtype=jnp.int32)
    same_owner = owners[:, None] == owners[None, :]
    earlier = req_order[None, :] < req_order[:, None]
    before_mine = same_owner & earlier
    starts = jnp.sum(jnp.where(before_mine, req_lens[None, :], 0), axis=1)
    slot_rank = jnp.sum(before_mine.astype(jnp.int32), axis=1)
    positions = req_lens.astype(jnp.float32)
    query_sum, keyval_sum = lax.psum((query_part, keyval_part), "attn")
    query_rows, keyval_rows = finish(query_sum, keyval_sum, positions, heads_loc, kv_loc)
    slot_hit = (owners[None, :] == my_index) & (
        slot_rank[None, :] == jnp.arange(CAP, dtype=jnp.int32)[:, None]
    )
    chosen = jnp.sum(jnp.where(slot_hit, req_order[None, :], 0), axis=1)
    present = jnp.any(slot_hit, axis=1)
    my_start = jnp.take(starts, chosen)
    my_len = jnp.where(present, jnp.take(req_lens, chosen), 0)
    query_mine = jnp.take(query_rows, chosen, axis=0)
    keyval_mine = jnp.take(keyval_rows, chosen, axis=0).reshape(CAP, 2, kv_loc, HD)
    cache_local = kv_cache[0]
    grouped = query_mine.reshape(CAP, kv_loc, group_size, HD)
    scores = (
        jnp.einsum("ckgd,skd->ckgs", grouped, cache_local[:, 0], preferred_element_type=jnp.float32)
        * score_scale
    )
    own_score = (
        jnp.einsum("ckgd,ckd->ckg", grouped, keyval_mine[:, 0], preferred_element_type=jnp.float32)
        * score_scale
    )
    slot_pos = jnp.arange(cache_local.shape[0], dtype=jnp.int32)
    live = (slot_pos[None, :] >= my_start[:, None]) & (
        slot_pos[None, :] < (my_start + my_len)[:, None]
    )
    live = live[:, None, None, :]
    row_max = jnp.maximum(jnp.max(jnp.where(live, scores, -jnp.inf), axis=-1), own_score)
    weights = jnp.where(live, jnp.exp(scores - row_max[..., None]), 0.0)
    own_weight = jnp.exp(own_score - row_max)
    total_weight = jnp.sum(weights, axis=-1) + own_weight
    probs = (weights / total_weight[..., None]).astype(jnp.bfloat16)
    own_prob = (own_weight / total_weight).astype(jnp.bfloat16)
    mixed = jnp.einsum(
        "ckgs,skd->ckgd", probs, cache_local[:, 1], preferred_element_type=jnp.float32
    )
    mixed = (
        mixed
        + own_prob.astype(jnp.float32)[..., None]
        * keyval_mine[:, 1].astype(jnp.float32)[:, :, None, :]
    )
    out_slots = mixed.reshape(CAP, heads_loc * HD).astype(jnp.bfloat16)
    gathered = lax.all_gather(out_slots, "attn", axis=0, tiled=True)
    heads_out = jnp.take(gathered, owners * CAP + slot_rank, axis=0)
    out_part = jnp.dot(heads_out, w_output, preferred_element_type=jnp.float32)
    out_total = lax.psum(out_part, "tensor")
    return out_total.astype(jnp.bfloat16)


def solution(mesh):
    placed = (
        P("dp", "attn"),
        P("attn", "tensor"),
        P("attn", None, "tensor"),
        P("tensor", "attn"),
        P("dp", "attn", None, "tensor", None),
        P("dp", None),
        P("dp", None, None),
    )
    return jax.shard_map(
        local, mesh=mesh, in_specs=placed, out_specs=P("dp", "attn"), check_vma=False
    )
```

profile of v0, /device:TPU:1, one launch (start us, length us, event | category | flops | bytes accessed | tf_op | source)
XLA Modules:
  0.0 454.5 jit_solution(9612542293275163695)
XLA Ops:
  6.5 0.0 copy-start
  6.5 1.2 copy-done
  7.8 1.0 convolution_bitcast_fusion
  8.8 0.0 copy-start.5
  8.8 0.0 copy-start.6
  8.8 1.2 copy.37
  10.0 0.0 copy-done.5
  10.0 0.0 copy-done.6
  10.0 0.2 fusion.30
  10.2 0.0 copy-start.4
  10.2 0.8 reshape.238
  11.0 0.0 all-reduce.3.cloned.1.call-update
  11.1 0.0 all-gather.3.cloned.1.call-start
  11.1 0.0 copy-done.1
  11.1 0.0 copy-done.7
  11.1 0.2 select_reduce_fusion.1
  11.3 0.1 select_reduce_fusion.2
  11.5 0.6 gather_fusion.4
  12.1 0.6 gather_fusion.3
  12.8 1.4 copy.65
  14.1 0.1 fusion.24
  14.3 0.1 fusion.17
  14.4 0.2 multiply_cosine_fusion
  14.6 269.9 %all-reduce.3.cloned.1.call-done = (f32[64,32,128]{2,1,0:T(8,128)}, f32[64,2,4,128]{3,2,1,0:T(4,128)}) async-done(((f32[64,32,128]{2,1,0:T(8,128)}, f32[64,2,4,128]{3,2,1,0:T(4,128)}), (f32[64,32,128]{2,1,0:T(8,128)}, f32[64,2,4,128]{3,2,1,0:T(4,128)})) %all-reduce.3.cloned.1.call-update) | async-done | bytes 1310736 | tf_op jit(solution)/shard_map/psum | solution.py:62
  284.5 1.0 slice_bitcast_fusion.4
  285.5 0.9 slice.87
  286.4 0.2 fusion.12
  286.6 0.1 pad_maximum_fusion.1
  286.7 0.1 reshape.239
  286.8 0.6 gather_fusion.1
  287.4 0.1 broadcast_select_fusion
  287.5 0.5 subtract_convert_fusion
  288.0 0.3 pad_maximum_fusion
  288.3 0.2 copy.66
  288.5 0.6 gather_fusion
  289.1 0.1 copy_select_fusion
  289.1 0.1 fusion.15
  289.3 0.1 copy-done.3
  289.4 0.4 select_reduce_fusion
  289.8 0.2 fusion.7
  290.0 0.3 fusion.2
  290.3 0.6 reshape.283
  290.9 0.0 all-gather.3.cloned.1.call-update
  291.0 136.5 %all-gather.3.cloned.1.call-done = bf16[64,3,4096]{2,1,0:T(4,128)(2,1)} async-done(((bf16[1,3,4096]{2,1,0:T(4,128)(2,1)}), bf16[64,3,4096]{2,1,0:T(4,128)(2,1)}) %all-gather.3.cloned.1.call-update) | async-done | bytes 1572880 | tf_op jit(solution)/shard_map/all_gather | solution.py:103
  427.5 3.1 reshape.284
  430.6 0.9 gather_fusion.2
  431.5 1.6 fusion.3
  433.1 14.6 %psum.23 = bf16[64,128]{1,0:T(8,128)(2,1)} all-reduce(f32[64,128]{1,0:T(8,128)S(1)} %fusion.3), channel_id=1, replica_groups=mesh['attn'=64,'dp'=4,'tensor'=2] {'tensor'}, use_global_device_ids=true, to_apply=%region_8.10 | all-reduce | flops 8192 | bytes 49152 | tf_op jit(solution)/shard_map/psum | solution.py:106
  (23 shorter events, 0.2 us)
Async XLA Ops:
  6.5 1.2 copy-start
  6.5 277.9 %all-reduce.3.cloned.1.call-start = ((), (), s32[]{:S(2)}) async-start(), calls=%async_computation.1 | async-start | bytes 2621440 | tf_op jit(solution)/shard_map/psum | solution.py:62
  8.8 1.2 copy-start.5
  8.8 1.2 copy-start.6
  10.0 1.1 copy-start.1
  10.0 1.2 copy-start.7
  10.2 2.6 copy-start.4
  11.1 416.4 %all-gather.3.cloned.1.call-start = ((), (), s32[]{:S(2)}) async-start(), calls=%async_computation | async-start | bytes 2129920 | tf_op jit(solution)/shard_map/all_gather | solution.py:103
  284.5 3.0 copy-start.2
  287.9 1.4 copy-start.3
Sparse Core Ops, SparseCore 0:
  11.2 273.2 all-reduce.2
  291.1 136.3 all-gather.2
where the time goes:
time: 455 us
  waiting for transfers between devices  406 us (89%)
  blocking collectives  14.6 us (3%)
  local copies, waits for them, and re-layouts  14 us (3%)
  between operations  13.7 us (3%)
    psum x1, waiting for transfers between devices, local(): query_sum, keyval_sum = lax.psum((query_part, keyval_part), 'attn')  270 us
    all_gather x1, waiting for transfers between devices, local(): gathered = lax.all_gather(out_slots, 'attn', axis=0, tiled=True)  137 us
    psum x1, blocking collectives, local(): out_total = lax.psum(out_part, 'tensor')  14.6 us
  transfers between devices with their start and end apart: 2, of which 2 were waited for; matrix products, arithmetic and copies ran while one was open for 1% of the time, Pallas kernels for 0%

commit v1 on v0

--- a/solution.py
+++ b/solution.py
@@ -100,7 +100,8 @@
         * keyval_mine[:, 1].astype(jnp.float32)[:, :, None, :]
     )
     out_slots = mixed.reshape(CAP, heads_loc * HD).astype(jnp.bfloat16)
-    gathered = lax.all_gather(out_slots, "attn", axis=0, tiled=True)
+    copies = jnp.concatenate([out_slots] * lax.axis_size("attn"), axis=0)
+    gathered = lax.all_to_all(copies, "attn", 0, 0, tiled=True)
     heads_out = jnp.take(gathered, owners * CAP + slot_rank, axis=0)
     out_part = jnp.dot(heads_out, w_output, preferred_element_type=jnp.float32)
     out_total = lax.psum(out_part, "tensor")

time: 455 us -> 422 us (0.927)
  waiting for transfers between devices: 406 us -> 352 us
  starting transfers between devices: 0.04 us -> 9.05 us
  local copies, waits for them, and re-layouts: 14 us -> 21.1 us
    all_gather x1 -> x0, waiting for transfers between devices: 137 us -> none  [local(): gathered = lax.all_gather(out_slots, 'attn', axis=0, tiled=True)]
    all_to_all x0 -> x1, waiting for transfers between devices: none -> 82.3 us  [local(): gathered = lax.all_to_all(copies, 'attn', 0, 0, tiled=True)]
    all_to_all x0 -> x1, starting transfers between devices: none -> 9.05 us  [local(): gathered = lax.all_to_all(copies, 'attn', 0, 0, tiled=True)]
    all_to_all x0 -> x2, local copies, waits for them, and re-layouts: none -> 5.49 us  [local(): gathered = lax.all_to_all(copies, 'attn', 0, 0, tiled=True)]
    concatenate x0 -> x1, local copies, waits for them, and re-layouts: none -> 5.31 us  [local(): copies = jnp.concatenate([out_slots] * lax.axis_size('attn'), axis=0)]
where the time goes in v1:
time: 422 us; the launch traced here: 421 us
  waiting for transfers between devices  352 us (83%)
  local copies, waits for them, and re-layouts  21.1 us (5%)
  blocking collectives  19.1 us (5%)
  between operations  13.7 us (3%)
  starting transfers between devices  9.05 us (2%)
    psum x1, waiting for transfers between devices, local(): query_sum, keyval_sum = lax.psum((query_part, keyval_part), 'attn')  270 us
    all_to_all x1, waiting for transfers between devices, local(): gathered = lax.all_to_all(copies, 'attn', 0, 0, tiled=True)  82.3 us
    psum x1, blocking collectives, local(): out_total = lax.psum(out_part, 'tensor')  19.1 us
    all_to_all x1, starting transfers between devices, local(): gathered = lax.all_to_all(copies, 'attn', 0, 0, tiled=True)  9.05 us
  transfers between devices with their start and end apart: 2, of which 2 were waited for; matrix products, arithmetic and copies ran while one was open for 1% of the time, Pallas kernels for 0%

profile of v1, /device:TPU:1, one launch (start us, length us, event | category | flops | bytes accessed | tf_op | source)
XLA Modules:
  0.0 421.0 jit_solution(2377793168393464195)
XLA Ops:
  6.5 0.0 copy-start
  6.5 0.0 all-reduce.3.cloned.1.call-start
  6.5 1.2 copy-done
  7.8 1.0 convolution_bitcast_fusion
  8.8 0.0 copy-start.5
  8.8 0.0 copy-start.6
  8.8 1.2 copy.31
  10.0 0.0 copy-done.5
  10.0 0.2 fusion.30
  10.2 0.0 copy-start.4
  10.2 0.8 reshape.240
  11.0 0.0 all-reduce.3.cloned.1.call-update
  11.1 0.0 copy-done.1
  11.1 0.0 copy-done.7
  11.1 0.2 select_reduce_fusion.1
  11.3 0.1 select_reduce_fusion.2
  11.4 0.6 gather_fusion.4
  12.1 0.6 gather_fusion.3
  12.7 1.4 copy.62
  14.1 0.1 fusion.24
  14.3 0.1 fusion.17
  14.3 0.2 multiply_cosine_fusion
  14.5 269.9 %all-reduce.3.cloned.1.call-done = (f32[64,32,128]{2,1,0:T(8,128)}, f32[64,2,4,128]{3,2,1,0:T(4,128)}) async-done(((f32[64,32,128]{2,1,0:T(8,128)}, f32[64,2,4,128]{3,2,1,0:T(4,128)}), (f32[64,32,128]{2,1,0:T(8,128)}, f32[64,2,4,128]{3,2,1,0:T(4,128)})) %all-reduce.3.cloned.1.call-update) | async-done | bytes 1310736 | tf_op jit(solution)/shard_map/psum | solution.py:62
  284.4 1.0 slice_bitcast_fusion.4
  285.4 0.9 slice.87
  286.4 0.2 fusion.12
  286.5 0.1 pad_maximum_fusion.1
  286.7 0.1 reshape.241
  286.8 0.6 gather_fusion.1
  287.3 0.1 broadcast_select_fusion
  287.4 0.5 subtract_convert_fusion
  287.9 0.3 pad_maximum_fusion
  288.2 0.2 copy.63
  288.4 0.6 gather_fusion
  289.0 0.1 copy_select_fusion
  289.1 0.1 fusion.15
  289.2 0.1 copy-done.3
  289.3 0.4 select_reduce_fusion
  289.7 0.2 fusion.7
  290.0 0.3 fusion.2
  290.3 5.3 %concatenate.26 = bf16[192,4096]{1,0:T(8,128)(2,1)S(1)} concatenate(bf16[3,4096]{1,0:T(4,128)(2,1)S(1)} %bitcast.137, bf16[3,4096]{1,0:T(4,128)(2,1)S(1)} %bitcast.169, bf16[3,4096]{1,0:T(4,128)(2,1)S(1)} %bitcast.108, bf16[3,4096]{1,0:T(4,128)(2,1)S(1)} %bitcast.109, bf16[3,4096]{1,0:T(4,128)(2,1)S(1)} %bitcast.110, bf16[3,4096]{1,0:T(4,128)(2,1)S(1)} %bitcast.111, ...), dimensions={0} | concatenate | bytes 3145728 | tf_op jit(solution)/shard_map/concatenate | solution.py:103
  295.6 2.3 all_to_all.8
  297.9 9.1 %all-to-all-start = ((bf16[64,3,4096]{2,1,0:T(4,128)(2,1)}), bf16[64,3,4096]{2,1,0:T(4,128)(2,1)}, u32[]{:S(2)}, u32[]{:S(2)}) async-start(bf16[64,3,4096]{2,1,0:T(4,128)(2,1)} %all_to_all.8), calls=%async_computation | async-start | bytes 4194304 | tf_op jit(solution)/shard_map/all_to_all | solution.py:104
  307.0 82.3 %all-to-all-done = bf16[64,3,4096]{2,1,0:T(4,128)(2,1)} async-done(((bf16[64,3,4096]{2,1,0:T(4,128)(2,1)}), bf16[64,3,4096]{2,1,0:T(4,128)(2,1)}, u32[]{:S(2)}, u32[]{:S(2)}) %all-to-all-start) | async-done | bytes 1572896 | tf_op jit(solution)/shard_map/all_to_all | solution.py:104
  389.4 3.1 all_to_all.10
  392.5 0.9 gather_fusion.2
  393.4 1.6 fusion.3
  395.0 19.1 %psum.23 = bf16[64,128]{1,0:T(8,128)(2,1)} all-reduce(f32[64,128]{1,0:T(8,128)S(1)} %fusion.3), channel_id=1, replica_groups=mesh['attn'=64,'dp'=4,'tensor'=2] {'tensor'}, use_global_device_ids=true, to_apply=%region_8.10 | all-reduce | flops 8192 | bytes 49152 | tf_op jit(solution)/shard_map/psum | solution.py:107
  (24 shorter events, 0.2 us)
Async XLA Ops:
  6.5 1.2 copy-start
  6.5 277.9 %all-reduce.3.cloned.1.call-start = ((), (), s32[]{:S(2)}) async-start(), calls=%async_computation.1 | async-start | bytes 2621440 | tf_op jit(solution)/shard_map/psum | solution.py:62
  8.8 1.2 copy-start.5
  8.8 1.2 copy-start.6
  10.0 1.1 copy-start.1
  10.0 1.1 copy-start.7
  10.2 2.5 copy-start.4
  284.4 3.0 copy-start.2
  287.9 1.4 copy-start.3
  297.9 91.4 %all-to-all-start = ((bf16[64,3,4096]{2,1,0:T(4,128)(2,1)}), bf16[64,3,4096]{2,1,0:T(4,128)(2,1)}, u32[]{:S(2)}, u32[]{:S(2)}) async-start(bf16[64,3,4096]{2,1,0:T(4,128)(2,1)} %all_to_all.8), calls=%async_computation | async-start | bytes 4194304 | tf_op jit(solution)/shard_map/all_to_all | solution.py:104
Sparse Core Ops, SparseCore 0:
  11.2 273.1 all-reduce.2
